TPU v7x, 32 devices: a whole 2x2x4 slice. The times are simulated.
32 devices in a mesh: groups: 2 (over y), head: 8 (over z, x), req: 2 (over core).
Axes of the slice: x: 2, y: 2, z: 4, core: 2. Of those that a mesh axis runs over, the one named last changes fastest.
Arguments:
- tokens: bfloat16 [2, 64, 2048], P('req', ('groups', 'head')), parts along dimension 1, may hold values from -4 to 4
- ssm_state: bfloat16 [2, 8, 128, 64, 128], P('req', 'groups', 'head'), parts along dimension 1, may hold values from -2 to 2
- conv_x_state: bfloat16 [2, 8, 3, 8192], P('req', 'groups', None, 'head'), parts along dimension 1, may hold values from -6 to 6
- conv_bc_state: bfloat16 [2, 8, 3, 2048], P('req', 'groups', None, 'head'), parts along dimension 1, may hold values from -6 to 6
- expert_ids: int32 [2, 64, 2], P('req', ('groups', 'head')), parts along dimension 1, may hold values from 0 to 7, all different within a row; in each aligned block of 4 rows (0 to 3, 4 to 7, ..., all dimensions but the last counted through in order) at most 2 rows name the same one
- mixer_gain: float32 [2048], replicated, may hold values from 0.5 to 1.5
- weight_xz: bfloat16 [2048, 16384], P(None, 'head'), may hold values from -0.125 to 0.125
- weight_bc: bfloat16 [2048, 2048], P(None, 'head'), may hold values from -0.125 to 0.125
- weight_delta: bfloat16 [2048, 128], P(None, 'head'), may hold values from -0.125 to 0.125
- delta_bias: float32 [128], P('head'), may hold values from -4 to -1
- decay_log: float32 [128], P('head'), may hold values from 0 to 2.8
- skip_gain: float32 [128], P('head'), may hold values from 0.5 to 1.5
- conv_x_kernel: float32 [4, 8192], P(None, 'head'), may hold values from -3 to 3
- conv_x_bias: float32 [8192], P('head'), may hold values from -3 to 3
- conv_bc_kernel: float32 [4, 2048], P(None, 'head'), may hold values from -3 to 3
- conv_bc_bias: float32 [2048], P('head'), may hold values from -3 to 3
- gated_gain: float32 [8192], P('head'), may hold values from 0.5 to 1.5
- weight_out: bfloat16 [8192, 2048], P('head'), may hold values from -0.0625 to 0.0625
- ffn_gain: float32 [2048], replicated, may hold values from 0.5 to 1.5
- router_weight: bfloat16 [2048, 8], replicated, may hold values from -0.125 to 0.125
- weight_up: bfloat16 [2048, 16384], P(None, 'head'), may hold values from -0.125 to 0.125
- weight_down: bfloat16 [16384, 2048], P('head'), may hold values from -0.125 to 0.125
Outputs:
- layer_out: bfloat16 [2, 64, 2048], P('req', ('groups', 'head')), parts along dimension 1
- new_state: bfloat16 [2, 8, 128, 64, 128], P('req', 'groups', 'head'), parts along dimension 1
- new_conv_x: bfloat16 [2, 8, 3, 8192], P('req', 'groups', None, 'head'), parts along dimension 1
- new_conv_bc: bfloat16 [2, 8, 3, 2048], P('req', 'groups', None, 'head'), parts along dimension 1
There are 2 independent parts, one for each index of `groups`. A program takes and returns all parts, laid end to end along the dimension named above; an argument that names none is the same for every part. Nothing has to cross between parts.
Inputs may be any that keep to these rules, and one draw needn't show every extreme that they name: `expert_ids`: each row names 2 different experts; in each aligned block of 4 rows no expert is named more than 2 times, and the bound is reached.
All inputs are finite; a program needn't handle non-finite values.
Results may differ from a plain program's by a relative error of at most 0.017.
Values may be sent and summed in bfloat16 or wider, within the bound.
No kernel may reach another device: no remote copies, remote signals or barrier semaphores. Data moves between devices by JAX's collectives and lax.ppermute only.
A program may use at most 128 MiB of HBM per device.

v0:
```python
import jax
import jax.numpy as jnp
from jax import lax
from jax.sharding import PartitionSpec as P

HEADS = 128
G = 8
EXPERTS = 8
TOP = 2
STEPS = 8
CAP = 2
eps = 1e-05
highest = lax.Precision.HIGHEST


def norm_rows(values, gain):
    mean_square = jnp.mean(values * values, axis=-1, keepdims=True)
    return values * lax.rsqrt(mean_square + eps) * gain


def causal_conv(past_rows, fresh_rows, kernel, offset):
    window = jnp.concatenate([past_rows, fresh_rows], axis=1)
    window_wide = window.astype(jnp.float32)
    fresh_count = fresh_rows.shape[1]
    running = offset + kernel[0] * window_wide[:, 0:fresh_count]
    for tap_index in range(1, kernel.shape[0]):
        running = running + kernel[tap_index] * window_wide[:, tap_index : tap_index + fresh_count]
    return (jax.nn.silu(running), window[:, fresh_count:])


def route_share(ffn_in, router_weight, chosen_ids):
    logits = jnp.dot(ffn_in, router_weight, preferred_element_type=jnp.float32)
    match_table = (chosen_ids[:, :, None] == jnp.arange(EXPERTS)[None, None, :]).astype(jnp.float32)
    picked = jnp.einsum("mke,me->mk", match_table, logits, precision=highest)
    first_weight = jax.nn.sigmoid(picked[:, 0] - picked[:, 1])
    return jnp.stack([first_weight, 1.0 - first_weight], axis=1)


def expert_hidden(rows_in, weight_up):
    return jnp.square(
        jnp.maximum(jnp.dot(rows_in, weight_up, preferred_element_type=jnp.float32), 0.0)
    ).astype(jnp.bfloat16)


def shards(
    tokens,
    ssm_state,
    conv_x_state,
    conv_bc_state,
    expert_ids,
    mixer_gain,
    weight_xz,
    weight_bc,
    weight_delta,
    delta_bias,
    decay_log,
    skip_gain,
    conv_x_kernel,
    conv_x_bias,
    conv_bc_kernel,
    conv_bc_bias,
    gated_gain,
    weight_out,
    ffn_gain,
    router_weight,
    weight_up,
    weight_down,
):
    head_count = lax.axis_size("head")
    my_index = lax.axis_index("head")
    tok_local = tokens.shape[1]
    width = tokens.shape[2]
    requests = ssm_state.shape[1]
    heads_local = ssm_state.shape[2]
    head_dim = ssm_state.shape[3]
    state_dim = ssm_state.shape[4]
    gathered = lax.all_gather(tokens, "head", axis=1, tiled=True)
    inputs = gathered.reshape(requests * STEPS, width)
    normed = norm_rows(inputs.astype(jnp.float32), mixer_gain).astype(jnp.bfloat16)
    proj_xz = jnp.dot(normed, weight_xz, preferred_element_type=jnp.float32).reshape(
        requests, STEPS, heads_local, 2, head_dim
    )
    x_fresh = (
        proj_xz[:, :, :, 0, :].reshape(requests, STEPS, heads_local * head_dim).astype(jnp.bfloat16)
    )
    z_gate = proj_xz[:, :, :, 1, :]
    bc_fresh = (
        jnp.dot(normed, weight_bc, preferred_element_type=jnp.float32)
        .reshape(requests, STEPS, -1)
        .astype(jnp.bfloat16)
    )
    delta = jax.nn.softplus(
        jnp.dot(normed, weight_delta, preferred_element_type=jnp.float32).reshape(
            requests, STEPS, heads_local
        )
        + delta_bias
    )
    x_conv, conv_x_new = causal_conv(conv_x_state[0], x_fresh, conv_x_kernel, conv_x_bias)
    bc_conv, conv_bc_new = causal_conv(conv_bc_state[0], bc_fresh, conv_bc_kernel, conv_bc_bias)
    bc_conv = bc_conv.astype(jnp.bfloat16)
    bc_all = lax.all_gather(bc_conv, "head", axis=2, tiled=True)
    bc_list = [bc_all[:, step_index] for step_index in range(STEPS)]
    head_global = my_index * heads_local + jnp.arange(heads_local)
    group_pick = (head_global[:, None] // (HEADS // G) == jnp.arange(G)[None, :]).astype(
        jnp.float32
    )
    x_heads = x_conv.reshape(requests, STEPS, heads_local, head_dim)
    decay_rate = jnp.exp(delta * -jnp.exp(decay_log))
    ssm_now = ssm_state[0]
    readings = []
    for step_index in range(STEPS):
        bc_values = bc_list[step_index].astype(jnp.float32).reshape(requests, 2, G, state_dim)
        b_heads = jnp.einsum("rgn,hg->rhn", bc_values[:, 0], group_pick, precision=highest)
        c_heads = jnp.einsum("rgn,hg->rhn", bc_values[:, 1], group_pick, precision=highest)
        x_step = x_heads[:, step_index]
        fresh_state = (
            decay_rate[:, step_index, :, None, None] * ssm_now.astype(jnp.float32)
            + (delta[:, step_index, :, None] * x_step)[..., None] * b_heads[:, :, None, :]
        )
        readings.append(
            jnp.einsum("rhpn,rhn->rhp", fresh_state, c_heads, precision=highest)
            + skip_gain[:, None] * x_step
        )
        ssm_now = fresh_state.astype(jnp.bfloat16)
    gated_out = jnp.stack(readings, axis=1) * jax.nn.silu(z_gate)
    group_normed = (
        norm_rows(gated_out, gated_gain.reshape(heads_local, head_dim))
        .astype(jnp.bfloat16)
        .reshape(requests * STEPS, heads_local * head_dim)
    )
    per_expert = head_count // EXPERTS
    mixer_out = lax.psum_scatter(
        jnp.dot(group_normed, weight_out, preferred_element_type=jnp.float32),
        "head",
        scatter_dimension=0,
        tiled=True,
    )
    residual = (tokens[0].astype(jnp.float32) + mixer_out).astype(jnp.bfloat16)
    ffn_in = norm_rows(residual.astype(jnp.float32), ffn_gain).astype(jnp.bfloat16)
    share = route_share(ffn_in, router_weight, expert_ids[0])
    chosen = expert_ids[0].reshape(-1)
    onehot = (chosen[:, None] == jnp.arange(EXPERTS)[None, :]).astype(jnp.int32)
    earlier = jnp.cumsum(onehot, axis=0) - onehot
    position = jnp.sum(earlier * onehot, axis=1)
    slot_index = chosen * CAP + position
    place = (jnp.arange(EXPERTS * CAP)[:, None] == slot_index[None, :]).astype(jnp.bfloat16)
    routed_rows = jnp.repeat(ffn_in, TOP, axis=0)
    packed = jnp.dot(place, routed_rows, preferred_element_type=jnp.float32).astype(jnp.bfloat16)
    outgoing = jnp.repeat(packed.reshape(EXPERTS, CAP, width), per_expert, axis=0)
    received = lax.all_to_all(outgoing, "head", split_axis=0, concat_axis=0, tiled=True)
    flat_rows = received.reshape(-1, width)
    hidden = expert_hidden(flat_rows, weight_up)
    computed = jnp.dot(hidden, weight_down, preferred_element_type=jnp.float32).reshape(
        received.shape[0], received.shape[1], width
    )
    returned = lax.all_to_all(
        computed.astype(jnp.bfloat16), "head", split_axis=0, concat_axis=0, tiled=True
    ).astype(computed.dtype)
    summed = (
        returned.reshape(EXPERTS, per_expert, CAP, width).sum(axis=1).reshape(EXPERTS * CAP, width)
    )
    per_route = jnp.dot(place.astype(jnp.float32).T, summed, precision=highest).reshape(
        tok_local, TOP, width
    )
    combined = jnp.sum(share[:, :, None] * per_route, axis=1)
    layer_out = (residual.astype(jnp.float32) + combined).astype(jnp.bfloat16)
    return (layer_out[None], ssm_now[None], conv_x_new[None], conv_bc_new[None])


def solution(mesh):
    return jax.shard_map(
        shards,
        mesh=mesh,
        in_specs=(
            P("req", ("groups", "head"), None),
            P("req", "groups", "head", None, None),
            P("req", "groups", None, "head"),
            P("req", "groups", None, "head"),
            P("req", ("groups", "head"), None),
            P(),
            P(None, "head"),
            P(None, "head"),
            P(None, "head"),
            P("head"),
            P("head"),
            P("head"),
            P(None, "head"),
            P("head"),
            P(None, "head"),
            P("head"),
            P("head"),
            P("head", None),
            P(),
            P(),
            P(None, "head"),
            P("head", None),
        ),
        out_specs=(
            P("req", ("groups", "head"), None),
            P("req", "groups", "head", None, None),
            P("req", "groups", None, "head"),
            P("req", "groups", None, "head"),
        ),
        check_vma=False,
    )
```

profile of v0, /device:TPU:0, one launch (start us, length us, event | category | flops | bytes accessed | tf_op | source)
XLA Modules:
  0.0 269.9 jit_solution(17759373759885222538)
XLA Ops:
  7.2 0.8 copy.187
  8.1 32.5 %all_gather.6 = bf16[1,32,2048]{2,0,1:T(2,128)(2,1)S(1)} all-gather(bf16[1,4,2048]{2,0,1:T(2,128)(2,1)S(1)} %copy.187), channel_id=1, replica_groups=mesh['groups'=2,'head'=8,'req'=2] {'head'}, dimensions={1}, use_global_device_ids=true | all-gather | bytes 147456 | tf_op jit(solution)/shard_map/all_gather | solution.py:77
  41.6 0.8 fusion.167
  42.4 1.0 convolution_convert_fusion.2
  44.2 30.5 %all_gather.7 = bf16[4,8,2048]{2,1,0:T(8,128)(2,1)S(1)} all-gather(bf16[4,8,256]{2,1,0:T(8,128)(2,1)S(1)} %multiply_convert_fusion.2), channel_id=1, replica_groups=mesh['groups'=2,'head'=8,'req'=2] {'head'}, dimensions={2}, use_global_device_ids=true | all-gather | bytes 147456 | tf_op jit(solution)/shard_map/all_gather | solution.py:101
  79.3 0.8 convolution_bitcast_fusion.3
  80.1 0.8 fusion.114
  82.5 0.8 convolution_bitcast_fusion.1
  83.2 0.8 fusion.112
  84.8 0.8 fusion.111
  85.6 12.4 %copy.190 = bf16[2048,2048]{0,1:T(8,128)(2,1)} copy(bf16[2048,2048]{1,0:T(8,128)(2,1)} %param.28) | data formatting | bytes 16777216 | tf_op args[6]
  98.0 7.2 %fusion.74 = f32[4,8,16,2,64]{4,1,3,2,0:T(8,128)S(1)} fusion(bf16[16,2,64,2048,1]{3,2,1,0,4:T(8,128)(2,1)} %bitcast.433, bf16[1,32,2048]{2,1,0:T(8,128)(2,1)S(1)} %get-tuple-element.41, f32[2048]{0:T(1024)S(1)} %copy-done.31, f32[32]{0:T(128)S(1)} %add_rsqrt_fusion.2), kind=kOutput, calls=%fused_computation.102 | convolution fusion | flops 268697600 | bytes 8790144 | tf_op jit(solution)/shard_map/dot_general | solution.py:80
  106.7 4.3 %fusion.24 = f32[4,16,1,64]{3,2,1,0:T(1,128)S(1)} fusion(f32[4,16,128,1]{2,3,1,0:T(1,128)} %bitcast.467, bf16[1,4,16,64,128]{4,3,2,1,0:T(8,128)(2,1)S(1)} %copy-done.1, f32[4,16,128]{2,1,0:T(8,128)S(1)} %convolution_bitcast_fusion.7, f32[4,16,64]{2,1,0:T(8,128)S(1)} %get-tuple-element.57, f32[4,16]{1,0:T(4,128)S(1)} %bitcast.496), kind=kOutput, calls=%fused_computation.43 | convolution fusion | flops 8388608 | bytes 1147136 | tf_op jit(solution)/shard_map/rhpn,rhn->rhp/dot_general | solution.py:121
  111.0 5.0 %fusion.22 = f32[4,16,1,64]{3,2,1,0:T(1,128)S(1)} fusion(f32[4,16,128,1]{2,3,1,0:T(1,128)} %bitcast.468, f32[4,16,128]{2,1,0:T(8,128)S(1)} %convolution_bitcast_fusion.6, f32[4,16,64]{2,1,0:T(8,128)S(1)} %get-tuple-element.56, f32[4,16]{1,0:T(4,128)S(1)} %bitcast.491, bf16[1,4,16,64,128]{4,3,2,1,0:T(8,128)(2,1)S(1)} %copy-done.1, ...), kind=kOutput, calls=%fused_computation.41 | convolution fusion | flops 11010048 | bytes 1196544 | tf_op jit(solution)/shard_map/rhpn,rhn->rhp/dot_general | solution.py:121
  116.0 5.3 %fusion.20 = f32[4,16,1,64]{3,2,1,0:T(1,128)S(1)} fusion(f32[4,16,128,1]{2,3,1,0:T(1,128)S(1)} %bitcast.469, f32[4,16,128]{2,1,0:T(8,128)S(1)} %convolution_bitcast_fusion.5, f32[4,16,64]{2,1,0:T(8,128)S(1)} %get-tuple-element.55, f32[4,16]{1,0:T(4,128)S(1)} %bitcast.487, f32[4,16,128]{2,1,0:T(8,128)S(1)} %convolution_bitcast_fusion.6, ...), kind=kOutput, calls=%fused_computation.38 | convolution fusion | flops 13631488 | bytes 1245952 | tf_op jit(solution)/shard_map/rhpn,rhn->rhp/dot_general | solution.py:121
  121.3 3.2 %fusion.17 = bf16[4,16,64,128]{3,2,1,0:T(8,128)(2,1)S(1)} fusion(f32[4,16,128]{2,1,0:T(8,128)S(1)} %convolution_bitcast_fusion.4, f32[4,16,64]{2,1,0:T(8,128)S(1)} %get-tuple-element.54, f32[4,16]{1,0:T(4,128)S(1)} %bitcast.484, f32[4,16,128]{2,1,0:T(8,128)S(1)} %convolution_bitcast_fusion.5, f32[4,16,64]{2,1,0:T(8,128)S(1)} %get-tuple-element.55, ...), kind=kLoop, calls=%fused_computation.34 | loop fusion | flops 10485760 | bytes 2294784 | tf_op jit(solution)/shard_map/convert_element_type | solution.py:124
  124.6 6.9 %fusion.18 = f32[4,16,1,64]{3,2,1,0:T(1,128)S(1)} fusion(f32[4,16,128,1]{2,3,1,0:T(1,128)S(1)} %bitcast.470, f32[4,16,128]{2,1,0:T(8,128)S(1)} %convolution_bitcast_fusion.4, f32[4,16,64]{2,1,0:T(8,128)S(1)} %get-tuple-element.54, f32[4,16]{1,0:T(4,128)S(1)} %bitcast.485, f32[4,16,128]{2,1,0:T(8,128)S(1)} %convolution_bitcast_fusion.5, ...), kind=kOutput, calls=%fused_computation.35 | convolution fusion | flops 16252928 | bytes 1295360 | tf_op jit(solution)/shard_map/rhpn,rhn->rhp/dot_general | solution.py:121
  131.5 3.6 %fusion.16 = f32[4,16,1,64]{3,2,1,0:T(1,128)S(1)} fusion(f32[4,16,128,1]{2,3,1,0:T(1,128)S(1)} %bitcast.471, bf16[4,16,64,128]{3,2,1,0:T(8,128)(2,1)S(1)} %fusion.17, f32[4,16,128]{2,1,0:T(8,128)S(1)} %copy-done.6, f32[4,16,64]{2,1,0:T(8,128)S(1)} %get-tuple-element.53, f32[4,16]{1,0:T(4,128)S(1)} %bitcast.515), kind=kOutput, calls=%fused_computation.32 | convolution fusion | flops 8388608 | bytes 1147136 | tf_op jit(solution)/shard_map/rhpn,rhn->rhp/dot_general | solution.py:121
  135.1 4.7 %fusion.14 = f32[4,16,1,64]{3,2,1,0:T(1,128)S(1)} fusion(f32[4,16,128,1]{2,3,1,0:T(1,128)S(1)} %bitcast.472, f32[4,16,128]{2,1,0:T(8,128)S(1)} %copy-done.8, f32[4,16,64]{2,1,0:T(8,128)S(1)} %get-tuple-element.52, f32[4,16]{1,0:T(4,128)S(1)} %bitcast.511, bf16[4,16,64,128]{3,2,1,0:T(8,128)(2,1)S(1)} %fusion.17, f32[4,16,128]{2,1,0:T(8,128)S(1)} %copy-done.6, ...), kind=kOutput, calls=%fused_computation.29 | convolution fusion | flops 11010048 | bytes 1196544 | tf_op jit(solution)/shard_map/rhpn,rhn->rhp/dot_general | solution.py:121
  139.9 5.3 %fusion.12 = f32[4,16,1,64]{3,2,1,0:T(1,128)S(1)} fusion(f32[4,16,128,1]{2,3,1,0:T(1,128)S(1)} %bitcast.473, f32[4,16,128]{2,1,0:T(8,128)S(1)} %copy-done.10, f32[4,16,64]{2,1,0:T(8,128)S(1)} %get-tuple-element.51, f32[4,16]{1,0:T(4,128)S(1)} %bitcast.508, f32[4,16,128]{2,1,0:T(8,128)S(1)} %copy-done.8, f32[4,16,64]{2,1,0:T(8,128)S(1)} %get-tuple-element.52, ...), kind=kOutput, calls=%fused_computation.26 | convolution fusion | flops 13631488 | bytes 1245952 | tf_op jit(solution)/shard_map/rhpn,rhn->rhp/dot_general | solution.py:121
  145.3 6.7 %fusion.6 = f32[4,16,1,64]{3,2,1,0:T(1,128)S(1)} fusion(f32[4,16,128,1]{2,3,1,0:T(1,128)S(1)} %bitcast.474, f32[4,16,128]{2,1,0:T(8,128)S(1)} %copy-done.12, f32[4,16,64]{2,1,0:T(8,128)S(1)} %get-tuple-element.50, f32[4,16]{1,0:T(4,128)S(1)} %bitcast.506, f32[4,16,128]{2,1,0:T(8,128)S(1)} %copy-done.10, f32[4,16,64]{2,1,0:T(8,128)S(1)} %get-tuple-element.51, ...), kind=kOutput, calls=%fused_computation.19 | convolution fusion | flops 16252928 | bytes 1295360 | tf_op jit(solution)/shard_map/rhpn,rhn->rhp/dot_general | solution.py:121
  152.5 0.8 fusion.70
  153.3 0.8 copy.219
  154.9 3.7 %fusion.84 = f32[32,2048]{1,0:T(8,128)} fusion(bf16[1024,2048]{1,0:T(8,128)(2,1)} %param.39, f32[32,1024]{1,0:T(8,128)S(1)} %mul.831, f32[32,1024]{1,0:T(8,128)S(1)} %stack.43, f32[32,1024]{1,0:T(8,128)S(1)} %squeeze.121, f32[1024]{0:T(1024)} %param.38), kind=kOutput, calls=%fused_computation.116 | convolution fusion | flops 134479872 | bytes 4853760 | tf_op jit(solution)/shard_map/dot_general | solution.py:133
  158.8 7.0 %add_convert_fusion = bf16[1,4,16,64,128]{4,3,2,1,0:T(8,128)(2,1)} fusion(bf16[1,4,16,64,128]{4,3,2,1,0:T(8,128)(2,1)S(1)} %copy-done.1, f32[4,16,128]{2,1,0:T(8,128)S(1)} %copy-done.13, f32[4,16,64]{2,1,0:T(8,128)S(1)} %get-tuple-element.50, f32[4,16,128]{2,1,0:T(8,128)S(1)} %copy-done.11, f32[4,16,64]{2,1,0:T(8,128)S(1)} %get-tuple-element.51, ...), kind=kLoop, calls=%fused_computation.12 | loop fusion | flops 20971520 | bytes 2492416 | tf_op jit(solution)/shard_map/convert_element_type | solution.py:124
  169.0 61.4 %all-reduce.3.cloned.1.call-done = f32[32,2048]{1,0:T(8,128)} async-done(((f32[32,2048]{1,0:T(8,128)}), f32[32,2048]{1,0:T(8,128)}) %all-reduce.3.cloned.1.call-update) | async-done | bytes 262160
  230.4 1.0 fusion.89
  232.5 3.9 %all-to-all-start = ((bf16[8,2,2048]{2,1,0:T(2,128)(2,1)}), bf16[8,2,2048]{2,1,0:T(2,128)(2,1)S(1)}, u32[]{:S(2)}, u32[]{:S(2)}) async-start(bf16[8,2,2048]{2,1,0:T(2,128)(2,1)} %reshape_broadcast_in_dim_reshape.3), calls=%async_computation | async-start | bytes 131072 | tf_op jit(solution)/shard_map/all_to_all | solution.py:150
  236.7 6.6 %all-to-all-done = bf16[8,2,2048]{2,1,0:T(2,128)(2,1)S(1)} async-done(((bf16[8,2,2048]{2,1,0:T(2,128)(2,1)}), bf16[8,2,2048]{2,1,0:T(2,128)(2,1)S(1)}, u32[]{:S(2)}, u32[]{:S(2)}) %all-to-all-start) | async-done | bytes 65568 | tf_op jit(solution)/shard_map/all_to_all | solution.py:150
  243.3 8.0 %convolution_convert_fusion.1 = bf16[16,2048]{1,0:T(8,128)(2,1)S(1)} fusion(bf16[2048,2048]{1,0:T(8,128)(2,1)} %param.43, bf16[16,2048]{1,0:T(8,128)(2,1)S(1)} %reshape.366, bf16[2048,2048]{1,0:T(8,128)(2,1)} %param.42), kind=kOutput, calls=%fused_computation.6 | convolution fusion | flops 268566528 | bytes 16908288 | tf_op jit(solution)/shard_map/dot_general | solution.py:153
  252.1 3.3 %all-to-all-start.1 = ((bf16[8,2,2048]{2,1,0:T(2,128)(2,1)}), bf16[8,2,2048]{2,1,0:T(2,128)(2,1)S(1)}, u32[]{:S(2)}, u32[]{:S(2)}) async-start(bf16[8,2,2048]{2,1,0:T(2,128)(2,1)} %convert_element_type.233), calls=%async_computation.1 | async-start | bytes 131072 | tf_op jit(solution)/shard_map/all_to_all | solution.py:156
  255.5 6.8 %all-to-all-done.1 = bf16[8,2,2048]{2,1,0:T(2,128)(2,1)S(1)} async-done(((bf16[8,2,2048]{2,1,0:T(2,128)(2,1)}), bf16[8,2,2048]{2,1,0:T(2,128)(2,1)S(1)}, u32[]{:S(2)}, u32[]{:S(2)}) %all-to-all-start.1) | async-done | bytes 65568 | tf_op jit(solution)/shard_map/all_to_all | solution.py:156
  (180 shorter events, 16.6 us)
Async XLA Ops:
  7.2 35.3 %copy-start = (bf16[2048,256]{1,0:T(8,128)(2,1)S(1)}, bf16[2048,256]{1,0:T(8,128)(2,1)}, u32[]{:S(2)}) copy-start(bf16[2048,256]{1,0:T(8,128)(2,1)} %param.29) | copy-start | bytes 3145732
  7.2 78.5 %copy-start.46 = (f32[16]{0:T(128)S(1)}, f32[16]{0:T(128)}, u32[]{:S(2)}) copy-start(f32[16]{0:T(128)} %param.32) | copy-start | bytes 196
  7.2 223.2 %all-reduce.3.cloned.1.call-start = ((), (), s32[]{:S(2)}) async-start(), calls=%async_computation.2 | async-start | bytes 524288
  85.6 12.4 %copy-start.31 = (f32[2048]{0:T(1024)S(1)}, f32[2048]{0:T(1024)}, u32[]{:S(2)}) copy-start(f32[2048]{0:T(1024)} %param.27) | copy-start | bytes 24580
  98.0 7.5 %copy-start.21 = (bf16[1,4,3,1024]{3,1,2,0:T(4,128)(2,1)S(1)}, bf16[1,4,3,1024]{3,1,2,0:T(4,128)(2,1)}, u32[]{:S(2)}) copy-start(bf16[1,4,3,1024]{3,1,2,0:T(4,128)(2,1)} %param.24) | copy-start | bytes 73732
  98.0 7.5 %copy-start.30 = (f32[4,1024]{1,0:T(4,128)S(1)}, f32[4,1024]{1,0:T(4,128)}, u32[]{:S(2)}) copy-start(f32[4,1024]{1,0:T(4,128)} %param.34) | copy-start | bytes 49156
  98.0 7.6 %copy-start.41 = (f32[1024]{0:T(1024)S(1)}, f32[1024]{0:T(1024)}, u32[]{:S(2)}) copy-start(f32[1024]{0:T(1024)} %param.35) | copy-start | bytes 12292
  106.4 18.1 %copy-start.22 = (f32[4,1,16]{2,1,0:T(1,128)}, f32[4,1,16]{2,1,0:T(1,128)S(1)}, u32[]{:S(2)}) copy-start(f32[4,1,16]{2,1,0:T(1,128)S(1)} %get-tuple-element.62) | copy-start | bytes 772
  106.4 18.1 %copy-start.24 = (f32[4,1,16]{2,1,0:T(1,128)}, f32[4,1,16]{2,1,0:T(1,128)S(1)}, u32[]{:S(2)}) copy-start(f32[4,1,16]{2,1,0:T(1,128)S(1)} %get-tuple-element.63) | copy-start | bytes 772
  106.4 18.1 %copy-start.26 = (f32[4,1,16]{2,1,0:T(1,128)}, f32[4,1,16]{2,1,0:T(1,128)S(1)}, u32[]{:S(2)}) copy-start(f32[4,1,16]{2,1,0:T(1,128)S(1)} %get-tuple-element.64) | copy-start | bytes 772
  106.4 18.1 %copy-start.28 = (f32[4,1,16]{2,1,0:T(1,128)}, f32[4,1,16]{2,1,0:T(1,128)S(1)}, u32[]{:S(2)}) copy-start(f32[4,1,16]{2,1,0:T(1,128)S(1)} %get-tuple-element.65) | copy-start | bytes 772
  106.5 38.7 %copy-start.32 = (f32[4,1,16]{2,1,0:T(1,128)}, f32[4,1,16]{2,1,0:T(1,128)S(1)}, u32[]{:S(2)}) copy-start(f32[4,1,16]{2,1,0:T(1,128)S(1)} %get-tuple-element.58) | copy-start | bytes 772
  106.5 38.7 %copy-start.34 = (f32[4,1,16]{2,1,0:T(1,128)}, f32[4,1,16]{2,1,0:T(1,128)S(1)}, u32[]{:S(2)}) copy-start(f32[4,1,16]{2,1,0:T(1,128)S(1)} %get-tuple-element.59) | copy-start | bytes 772
  106.5 38.7 %copy-start.36 = (f32[4,1,16]{2,1,0:T(1,128)}, f32[4,1,16]{2,1,0:T(1,128)S(1)}, u32[]{:S(2)}) copy-start(f32[4,1,16]{2,1,0:T(1,128)S(1)} %get-tuple-element.60) | copy-start | bytes 772
  106.5 38.7 %copy-start.38 = (f32[4,1,16]{2,1,0:T(1,128)}, f32[4,1,16]{2,1,0:T(1,128)S(1)}, u32[]{:S(2)}) copy-start(f32[4,1,16]{2,1,0:T(1,128)S(1)} %get-tuple-element.61) | copy-start | bytes 772
  106.6 38.6 %copy-start.2 = (f32[4,16,64]{2,1,0:T(8,128)}, f32[4,16,64]{2,1,0:T(8,128)S(1)}, u32[]{:S(2)}) copy-start(f32[4,16,64]{2,1,0:T(8,128)S(1)} %get-tuple-element.52) | copy-start | bytes 49156
  106.6 38.6 %copy-start.4 = (f32[4,16,64]{2,1,0:T(8,128)}, f32[4,16,64]{2,1,0:T(8,128)S(1)}, u32[]{:S(2)}) copy-start(f32[4,16,64]{2,1,0:T(8,128)S(1)} %get-tuple-element.53) | copy-start | bytes 49156
  111.0 5.0 %copy-start.15 = (f32[16,4,128]{2,0,1:T(8,128)S(1)}, f32[16,4,128]{2,0,1:T(8,128)}, u32[]{:S(2)}) copy-start(f32[16,4,128]{2,0,1:T(8,128)} %fusion.116) | copy-start | bytes 98308
  124.6 6.9 %copy-start.6 = (f32[4,16,128]{2,1,0:T(8,128)S(1)}, f32[4,16,128]{2,1,0:T(8,128)}, u32[]{:S(2)}) copy-start(f32[4,16,128]{2,1,0:T(8,128)} %convolution_bitcast_fusion.3) | copy-start | bytes 98308
  124.6 6.9 %copy-start.17 = (f32[16,4,128]{2,0,1:T(8,128)S(1)}, f32[16,4,128]{2,0,1:T(8,128)}, u32[]{:S(2)}) copy-start(f32[16,4,128]{2,0,1:T(8,128)} %fusion.114) | copy-start | bytes 98308
  135.1 4.7 %copy-start.10 = (f32[4,16,128]{2,1,0:T(8,128)S(1)}, f32[4,16,128]{2,1,0:T(8,128)}, u32[]{:S(2)}) copy-start(f32[4,16,128]{2,1,0:T(8,128)} %convolution_bitcast_fusion.1) | copy-start | bytes 98308
  135.1 4.7 %copy-start.19 = (f32[16,4,128]{2,0,1:T(8,128)S(1)}, f32[16,4,128]{2,0,1:T(8,128)}, u32[]{:S(2)}) copy-start(f32[16,4,128]{2,0,1:T(8,128)} %fusion.112) | copy-start | bytes 98308
  139.8 5.4 %copy-start.12 = (f32[4,16,128]{2,1,0:T(8,128)S(1)}, f32[4,16,128]{2,1,0:T(8,128)}, u32[]{:S(2)}) copy-start(f32[4,16,128]{2,1,0:T(8,128)} %convolution_bitcast_fusion) | copy-start | bytes 98308
  139.8 5.4 %copy-start.20 = (f32[16,4,128]{2,0,1:T(8,128)S(1)}, f32[16,4,128]{2,0,1:T(8,128)}, u32[]{:S(2)}) copy-start(f32[16,4,128]{2,0,1:T(8,128)} %fusion.111) | copy-start | bytes 98308
  145.2 6.7 %copy-start.43 = (f32[16]{0:T(128)S(1)}, f32[16]{0:T(128)}, u32[]{:S(2)}) copy-start(f32[16]{0:T(128)} %param.33) | copy-start | bytes 196
  158.6 7.2 %copy-start.42 = (s32[1,4,2]{1,2,0:T(2,128)S(1)}, s32[1,4,2]{1,2,0:T(2,128)}, u32[]{:S(2)}) copy-start(s32[1,4,2]{1,2,0:T(2,128)} %param.26) | copy-start | bytes 100
  158.6 9.1 %copy-start.48 = (u32[32]{0:T(128)S(1)}, u32[32]{0:T(128)}, u32[]{:S(2)}) copy-start(u32[32]{0:T(128)} %constant.62) | copy-start | bytes 388
  158.6 71.8 %copy-start.14 = (bf16[1,4,2048]{2,1,0:T(4,128)(2,1)S(1)}, bf16[1,4,2048]{2,1,0:T(4,128)(2,1)}, u32[]{:S(2)}) copy-start(bf16[1,4,2048]{2,1,0:T(4,128)(2,1)} %param.22) | copy-start | bytes 49156
  158.6 72.8 %copy-start.40 = (f32[2048]{0:T(1024)S(1)}, f32[2048]{0:T(1024)}, u32[]{:S(2)}) copy-start(f32[2048]{0:T(1024)} %param.40) | copy-start | bytes 24580
  158.6 72.9 %copy-start.45 = (bf16[2048,8]{0,1:T(8,128)(2,1)S(1)}, bf16[2048,8]{0,1:T(8,128)(2,1)}, u32[]{:S(2)}) copy-start(bf16[2048,8]{0,1:T(8,128)(2,1)} %param.41) | copy-start | bytes 98308
  232.5 10.8 %all-to-all-start = ((bf16[8,2,2048]{2,1,0:T(2,128)(2,1)}), bf16[8,2,2048]{2,1,0:T(2,128)(2,1)S(1)}, u32[]{:S(2)}, u32[]{:S(2)}) async-start(bf16[8,2,2048]{2,1,0:T(2,128)(2,1)} %reshape_broadcast_in_dim_reshape.3), calls=%async_computation | async-start | bytes 131072 | tf_op jit(solution)/shard_map/all_to_all | solution.py:150
  252.1 10.2 %all-to-all-start.1 = ((bf16[8,2,2048]{2,1,0:T(2,128)(2,1)}), bf16[8,2,2048]{2,1,0:T(2,128)(2,1)S(1)}, u32[]{:S(2)}, u32[]{:S(2)}) async-start(bf16[8,2,2048]{2,1,0:T(2,128)(2,1)} %convert_element_type.233), calls=%async_computation.1 | async-start | bytes 131072 | tf_op jit(solution)/shard_map/all_to_all | solution.py:156
  (20 other events, 68.3 us)
Sparse Core Ops, SparseCore 0:
  158.8 71.5 all-reduce.2
where the time goes:
time: 271 us; the launch traced here: 270 us
  waiting for transfers between devices  74.9 us (28%)
  matrix products  72.9 us (27%)
  blocking collectives  63 us (23%)
  local copies, waits for them, and re-layouts  21.8 us (8%)
  between operations  15.6 us (6%)
  other arithmetic  14.4 us (5%)
  starting transfers between devices  7.28 us (3%)
    unnamed x2, waiting for transfers between devices  61.4 us
    dot_general x8, matrix products, shards(): jnp.einsum('rhpn,rhn->rhp', fresh_state, c_heads, precision=highest)  41.8 us
    all_gather x1, blocking collectives, shards(): gathered = lax.all_gather(tokens, 'head', axis=1, tiled=True)  32.5 us
    all_gather x1, blocking collectives, shards(): bc_all = lax.all_gather(bc_conv, 'head', axis=2, tiled=True)  30.5 us
    unnamed x114, local copies, waits for them, and re-layouts  16.2 us
    convert_element_type x2, other arithmetic, shards(): ssm_now = fresh_state.astype(jnp.bfloat16)  10.2 us
    dot_general x1, matrix products, shards(): jnp.dot(hidden, weight_down, preferred_element_type=jnp.float32)  8.05 us
    dot_general x1, matrix products, shards(): jnp.dot(normed, weight_xz, preferred_element_type=jnp.float32)  7.21 us
  transfers between devices with their start and end apart: 3, of which 3 were waited for; matrix products, arithmetic and copies ran while one was open for 4% of the time, Pallas kernels for 0%

commit v1 on v0

--- a/solution.py
+++ b/solution.py
@@ -11,6 +11,28 @@
 CAP = 2
 eps = 1e-05
 highest = lax.Precision.HIGHEST
+
+
+def laid_out(blocks, dim):
+    blocks = jnp.moveaxis(blocks, 0, dim)
+    dims = blocks.shape
+    return blocks.reshape(*dims[:dim], dims[dim] * dims[dim + 1], *dims[dim + 2 :])
+
+
+def collect(x, axis, dim):
+    size = lax.axis_size(axis)
+    pairs = [(i, (i + 1) % size) for i in range(size)]
+    back = [(b, a) for a, b in pairs]
+    lower, upper = ([], [])
+    for lap in range(size - 1):
+        if lap % 2 == 0:
+            lower.append(lax.ppermute(lower[-1] if lower else x, axis, pairs))
+        else:
+            upper.append(lax.ppermute(upper[-1] if upper else x, axis, back))
+    pieces = jnp.stack([*lower[::-1], x, *upper])
+    shift = lax.axis_index(axis) - len(lower)
+    pieces = pieces[(jnp.arange(size) - shift) % size]
+    return laid_out(pieces, dim)
 
 
 def norm_rows(values, gain):
@@ -74,7 +96,7 @@
     heads_local = ssm_state.shape[2]
     head_dim = ssm_state.shape[3]
     state_dim = ssm_state.shape[4]
-    gathered = lax.all_gather(tokens, "head", axis=1, tiled=True)
+    gathered = collect(tokens, "head", 1)
     inputs = gathered.reshape(requests * STEPS, width)
     normed = norm_rows(inputs.astype(jnp.float32), mixer_gain).astype(jnp.bfloat16)
     proj_xz = jnp.dot(normed, weight_xz, preferred_element_type=jnp.float32).reshape(

time: 271 us -> 272 us (level)
  blocking collectives: 63 us -> 30.8 us
  waiting for transfers between devices: 74.9 us -> 93.8 us
  starting transfers between devices: 7.28 us -> 22.9 us
    all_gather x1 -> x0, blocking collectives: 32.5 us -> none  [shards(): gathered = lax.all_gather(tokens, 'head', axis=1, tiled=True)]
    ppermute x0 -> x7, starting transfers between devices: none -> 15.6 us  [the longest x3 12.6 us: collect(): upper.append(lax.ppermute(upper[-1] if upper else x, axis, back))]
    unnamed x2, waiting for transfers between devices: 61.4 us -> 71 us
    ppermute x0 -> x7, waiting for transfers between devices: none -> 9.37 us  [the longest x4 8.07 us: collect(): lower.append(lax.ppermute(lower[-1] if lower else x, axis, pairs))]
    unnamed x114 -> x80, local copies, waits for them, and re-layouts: 16.2 us -> 15.2 us
  transfers between devices with their start and end apart: 3 -> 10, of which waited for: 3 -> 6; matrix products, arithmetic and copies ran while one was open for 4% -> 7% of each run, Pallas kernels for 0% -> 0%
where the time goes in v1:
time: 272 us
  waiting for transfers between devices  93.8 us (34%)
  matrix products  71.5 us (26%)
  blocking collectives  30.8 us (11%)
  starting transfers between devices  22.9 us (8%)
  local copies, waits for them, and re-layouts  22.8 us (8%)
  between operations  15.4 us (6%)
  other arithmetic  14.4 us (5%)
    unnamed x2, waiting for transfers between devices  71 us
    dot_general x8, matrix products, shards(): jnp.einsum('rhpn,rhn->rhp', fresh_state, c_heads, precision=highest)  41.4 us
    all_gather x1, blocking collectives, shards(): bc_all = lax.all_gather(bc_conv, 'head', axis=2, tiled=True)  30.8 us
    unnamed x80, local copies, waits for them, and re-layouts  15.2 us
    ppermute x3, starting transfers between devices, collect(): upper.append(lax.ppermute(upper[-1] if upper else x, axis, back))  12.6 us
    convert_element_type x2, other arithmetic, shards(): ssm_now = fresh_state.astype(jnp.bfloat16)  10.2 us
    ppermute x4, waiting for transfers between devices, collect(): lower.append(lax.ppermute(lower[-1] if lower else x, axis, pairs))  8.07 us
    dot_general x1, matrix products, shards(): jnp.dot(hidden, weight_down, preferred_element_type=jnp.float32)  8.05 us
  transfers between devices with their start and end apart: 10, of which 6 were waited for; matrix products, arithmetic and copies ran while one was open for 7% of the time, Pallas kernels for 0%

profile of v1, /device:TPU:0, one launch (start us, length us, event | category | flops | bytes accessed | tf_op | source)
XLA Modules:
  0.0 271.6 jit_solution(6247793713937820430)
XLA Ops:
  7.2 3.0 %collective-permute-start = (bf16[1,4,2048]{2,1,0:T(4,128)(2,1)}, bf16[1,4,2048]{2,1,0:T(4,128)(2,1)S(1)}, u32[]{:S(2)}, u32[]{:S(2)}) collective-permute-start(bf16[1,4,2048]{2,1,0:T(4,128)(2,1)} %param.22), channel_id=1, source_target_pairs={{0,2},{2,4},{4,6},{6,8},{8,10},{10,12},{12,14},{14,0},{1,3},{3,5},... | collective-permute-start | bytes 49160 | tf_op jit(solution)/shard_map/ppermute | solution.py:29
  10.2 3.1 %collective-permute-start.4 = (bf16[1,4,2048]{2,1,0:T(4,128)(2,1)}, bf16[1,4,2048]{2,1,0:T(4,128)(2,1)S(1)}, u32[]{:S(2)}, u32[]{:S(2)}) collective-permute-start(bf16[1,4,2048]{2,1,0:T(4,128)(2,1)} %param.22), channel_id=1, source_target_pairs={{2,0},{4,2},{6,4},{8,6},{10,8},{12,10},{14,12},{0,14},{3,1},{5,3},... | collective-permute-start | bytes 49160 | tf_op jit(solution)/shard_map/ppermute | solution.py:31
  13.3 0.9 fusion.158
  14.2 0.8 fusion.159
  16.3 1.2 exponential_negate_fusion
  17.5 6.4 %collective-permute-done.1 = bf16[1,4,2048]{2,1,0:T(4,128)(2,1)S(1)} collective-permute-done((bf16[1,4,2048]{2,1,0:T(4,128)(2,1)S(1)}, bf16[1,4,2048]{2,1,0:T(4,128)(2,1)S(1)}, u32[]{:S(2)}, u32[]{:S(2)}) %collective-permute-start.1) | collective-permute-done | bytes 16416 | tf_op jit(solution)/shard_map/ppermute | solution.py:29
  23.9 4.8 %collective-permute-start.5 = (bf16[1,4,2048]{2,1,0:T(4,128)(2,1)S(1)}, bf16[1,4,2048]{2,1,0:T(4,128)(2,1)S(1)}, u32[]{:S(2)}, u32[]{:S(2)}) collective-permute-start(bf16[1,4,2048]{2,1,0:T(4,128)(2,1)S(1)} %collective-permute-done.4), channel_id=1, source_target_pairs={{2,0},{4,2},{6,4},{8,6},{10,8},{12,10},{14,12},{0,14},{3,1},{5,3},... | collective-permute-start | bytes 49160 | tf_op jit(solution)/shard_map/ppermute | solution.py:31
  28.7 1.6 collective-permute-done.2
  30.4 12.3 %copy.147 = bf16[2048,2048]{0,1:T(8,128)(2,1)} copy(bf16[2048,2048]{1,0:T(8,128)(2,1)} %param.28) | data formatting | bytes 16777216 | tf_op args[6]
  45.3 4.8 %collective-permute-start.6 = (bf16[1,4,2048]{2,1,0:T(4,128)(2,1)S(1)}, bf16[1,4,2048]{2,1,0:T(4,128)(2,1)S(1)}, u32[]{:S(2)}, u32[]{:S(2)}) collective-permute-start(bf16[1,4,2048]{2,1,0:T(4,128)(2,1)S(1)} %collective-permute-done.5), channel_id=1, source_target_pairs={{2,0},{4,2},{6,4},{8,6},{10,8},{12,10},{14,12},{0,14},{3,1},{5,3},... | collective-permute-start | bytes 49160 | tf_op jit(solution)/shard_map/ppermute | solution.py:31
  50.2 1.3 collective-permute-done.6
  53.0 30.8 %all_gather.3 = bf16[4,8,2048]{2,1,0:T(8,128)(2,1)S(1)} all-gather(bf16[4,8,256]{2,1,0:T(8,128)(2,1)S(1)} %multiply_convert_fusion.3), channel_id=1, replica_groups=mesh['groups'=2,'head'=8,'req'=2] {'head'}, dimensions={2}, use_global_device_ids=true | all-gather | bytes 147456 | tf_op jit(solution)/shard_map/all_gather | solution.py:123
  93.6 7.2 %fusion.74 = f32[4,8,16,2,64]{4,1,3,2,0:T(8,128)S(1)} fusion(bf16[16,2,64,2048,1]{3,2,1,0,4:T(8,128)(2,1)} %bitcast.445, bf16[4,8,2048,1,1]{2,1,0,3,4:T(8,128)(2,1)S(1)} %reshape.465), kind=kOutput, calls=%fused_computation.108 | convolution fusion | flops 268435456 | bytes 8781824 | tf_op jit(solution)/shard_map/dot_general | solution.py:102
  101.4 1.1 multiply_exponential_fusion
  102.8 4.3 %fusion.24 = f32[4,16,1,64]{3,2,1,0:T(1,128)S(1)} fusion(f32[4,16,128,1]{2,3,1,0:T(1,128)} %bitcast.480, bf16[1,4,16,64,128]{4,3,2,1,0:T(8,128)(2,1)S(1)} %copy-done.1, f32[4,16,128]{2,1,0:T(8,128)S(1)} %convolution_bitcast_fusion.7, f32[4,16,64]{2,1,0:T(8,128)S(1)} %get-tuple-element.51, f32[4,16]{1,0:T(4,128)S(1)} %bitcast.509), kind=kOutput, calls=%fused_computation.44 | convolution fusion | flops 8388608 | bytes 1147136 | tf_op jit(solution)/shard_map/rhpn,rhn->rhp/dot_general | solution.py:143
  107.1 4.9 %fusion.22 = f32[4,16,1,64]{3,2,1,0:T(1,128)S(1)} fusion(f32[4,16,128,1]{2,3,1,0:T(1,128)S(1)} %bitcast.482, f32[4,16,128]{2,1,0:T(8,128)S(1)} %convolution_bitcast_fusion.6, f32[4,16,64]{2,1,0:T(8,128)S(1)} %get-tuple-element.50, f32[4,16]{1,0:T(4,128)S(1)} %bitcast.504, bf16[1,4,16,64,128]{4,3,2,1,0:T(8,128)(2,1)S(1)} %copy-done.1, ...), kind=kOutput, calls=%fused_computation.42 | convolution fusion | flops 11010048 | bytes 1196544 | tf_op jit(solution)/shard_map/rhpn,rhn->rhp/dot_general | solution.py:143
  112.0 5.3 %fusion.20 = f32[4,16,1,64]{3,2,1,0:T(1,128)S(1)} fusion(f32[4,16,128,1]{2,3,1,0:T(1,128)S(1)} %bitcast.483, f32[4,16,128]{2,1,0:T(8,128)S(1)} %convolution_bitcast_fusion.5, f32[4,16,64]{2,1,0:T(8,128)S(1)} %get-tuple-element.49, f32[4,16]{1,0:T(4,128)S(1)} %bitcast.500, f32[4,16,128]{2,1,0:T(8,128)S(1)} %convolution_bitcast_fusion.6, ...), kind=kOutput, calls=%fused_computation.39 | convolution fusion | flops 13631488 | bytes 1245952 | tf_op jit(solution)/shard_map/rhpn,rhn->rhp/dot_general | solution.py:143
  117.3 3.2 %fusion.17 = bf16[4,16,64,128]{3,2,1,0:T(8,128)(2,1)S(1)} fusion(f32[4,16,128]{2,1,0:T(8,128)S(1)} %convolution_bitcast_fusion.4, f32[4,16,64]{2,1,0:T(8,128)S(1)} %get-tuple-element.48, f32[4,16]{1,0:T(4,128)S(1)} %bitcast.497, f32[4,16,128]{2,1,0:T(8,128)S(1)} %convolution_bitcast_fusion.5, f32[4,16,64]{2,1,0:T(8,128)S(1)} %get-tuple-element.49, ...), kind=kLoop, calls=%fused_computation.35 | loop fusion | flops 10485760 | bytes 2294784 | tf_op jit(solution)/shard_map/convert_element_type | solution.py:146
  120.5 6.7 %fusion.18 = f32[4,16,1,64]{3,2,1,0:T(1,128)S(1)} fusion(f32[4,16,128,1]{2,3,1,0:T(1,128)S(1)} %bitcast.484, f32[4,16,128]{2,1,0:T(8,128)S(1)} %convolution_bitcast_fusion.4, f32[4,16,64]{2,1,0:T(8,128)S(1)} %get-tuple-element.48, f32[4,16]{1,0:T(4,128)S(1)} %bitcast.498, f32[4,16,128]{2,1,0:T(8,128)S(1)} %convolution_bitcast_fusion.5, ...), kind=kOutput, calls=%fused_computation.36 | convolution fusion | flops 16252928 | bytes 1295360 | tf_op jit(solution)/shard_map/rhpn,rhn->rhp/dot_general | solution.py:143
  127.2 3.6 %fusion.16 = f32[4,16,1,64]{3,2,1,0:T(1,128)S(1)} fusion(f32[4,16,128,1]{2,3,1,0:T(1,128)S(1)} %bitcast.485, bf16[4,16,64,128]{3,2,1,0:T(8,128)(2,1)S(1)} %fusion.17, f32[4,16,128]{2,1,0:T(8,128)S(1)} %convolution_bitcast_fusion.3, f32[4,16,64]{2,1,0:T(8,128)S(1)} %get-tuple-element.47, f32[4,16]{1,0:T(4,128)S(1)} %bitcast.528), kind=kOutput, calls=%fused_computation.33 | convolution fusion | flops 8388608 | bytes 1147136 | tf_op jit(solution)/shard_map/rhpn,rhn->rhp/dot_general | solution.py:143
  130.8 4.7 %fusion.14 = f32[4,16,1,64]{3,2,1,0:T(1,128)S(1)} fusion(f32[4,16,128,1]{2,3,1,0:T(1,128)S(1)} %bitcast.486, f32[4,16,128]{2,1,0:T(8,128)S(1)} %convolution_bitcast_fusion.2, f32[4,16,64]{2,1,0:T(8,128)S(1)} %get-tuple-element.46, f32[4,16]{1,0:T(4,128)S(1)} %bitcast.524, bf16[4,16,64,128]{3,2,1,0:T(8,128)(2,1)S(1)} %fusion.17, ...), kind=kOutput, calls=%fused_computation.30 | convolution fusion | flops 11010048 | bytes 1196544 | tf_op jit(solution)/shard_map/rhpn,rhn->rhp/dot_general | solution.py:143
  135.5 5.3 %fusion.12 = f32[4,16,1,64]{3,2,1,0:T(1,128)S(1)} fusion(f32[4,16,128,1]{2,3,1,0:T(1,128)S(1)} %bitcast.487, f32[4,16,128]{2,1,0:T(8,128)S(1)} %copy-done.2, f32[4,16,64]{2,1,0:T(8,128)S(1)} %get-tuple-element.45, f32[4,16]{1,0:T(4,128)S(1)} %bitcast.521, f32[4,16,128]{2,1,0:T(8,128)S(1)} %convolution_bitcast_fusion.2, ...), kind=kOutput, calls=%fused_computation.27 | convolution fusion | flops 13631488 | bytes 1245952 | tf_op jit(solution)/shard_map/rhpn,rhn->rhp/dot_general | solution.py:143
  140.9 7.0 %add_convert_fusion = bf16[1,4,16,64,128]{4,3,2,1,0:T(8,128)(2,1)} fusion(bf16[1,4,16,64,128]{4,3,2,1,0:T(8,128)(2,1)S(1)} %copy-done.1, f32[4,16,128]{2,1,0:T(8,128)S(1)} %copy-done.3, f32[4,16,64]{2,1,0:T(8,128)S(1)} %get-tuple-element.44, f32[4,16,128]{2,1,0:T(8,128)S(1)} %copy-done.2, f32[4,16,64]{2,1,0:T(8,128)S(1)} %get-tuple-element.45, ...), kind=kLoop, calls=%fused_computation.13 | loop fusion | flops 20971520 | bytes 2492416 | tf_op jit(solution)/shard_map/convert_element_type | solution.py:146
  147.9 6.7 %fusion.6 = f32[4,16,1,64]{3,2,1,0:T(1,128)S(1)} fusion(f32[4,16,128,1]{2,3,1,0:T(1,128)S(1)} %bitcast.481, f32[4,16,128]{2,1,0:T(8,128)S(1)} %copy-done.3, f32[4,16,64]{2,1,0:T(8,128)S(1)} %get-tuple-element.44, f32[4,16]{1,0:T(4,128)S(1)} %bitcast.520, f32[4,16,128]{2,1,0:T(8,128)S(1)} %copy-done.2, f32[4,16,64]{2,1,0:T(8,128)S(1)} %get-tuple-element.45, ...), kind=kOutput, calls=%fused_computation.20 | convolution fusion | flops 16252928 | bytes 1295360 | tf_op jit(solution)/shard_map/rhpn,rhn->rhp/dot_general | solution.py:143
  156.1 3.7 %fusion.76 = f32[32,2048]{1,0:T(8,128)} fusion(bf16[1024,2048]{1,0:T(8,128)(2,1)} %param.39, f32[32,1024]{1,0:T(8,128)S(1)} %mul.853, f32[32,1024]{1,0:T(8,128)S(1)} %stack.79, f32[32,1024]{1,0:T(8,128)S(1)} %squeeze.121, f32[1024]{0:T(1024)S(1)} %copy-done.21), kind=kOutput, calls=%fused_computation.112 | convolution fusion | flops 134479872 | bytes 4853760 | tf_op jit(solution)/shard_map/dot_general | solution.py:155
  161.1 71.0 %all-reduce.3.cloned.1.call-done = f32[32,2048]{1,0:T(8,128)} async-done(((f32[32,2048]{1,0:T(8,128)}), f32[32,2048]{1,0:T(8,128)}) %all-reduce.3.cloned.1.call-update) | async-done | bytes 262160
  232.1 1.0 fusion.81
  234.2 3.9 %all-to-all-start = ((bf16[8,2,2048]{2,1,0:T(2,128)(2,1)}), bf16[8,2,2048]{2,1,0:T(2,128)(2,1)S(1)}, u32[]{:S(2)}, u32[]{:S(2)}) async-start(bf16[8,2,2048]{2,1,0:T(2,128)(2,1)} %reshape_broadcast_in_dim_reshape.3), calls=%async_computation | async-start | bytes 131072 | tf_op jit(solution)/shard_map/all_to_all | solution.py:172
  238.4 6.6 %all-to-all-done = bf16[8,2,2048]{2,1,0:T(2,128)(2,1)S(1)} async-done(((bf16[8,2,2048]{2,1,0:T(2,128)(2,1)}), bf16[8,2,2048]{2,1,0:T(2,128)(2,1)S(1)}, u32[]{:S(2)}, u32[]{:S(2)}) %all-to-all-start) | async-done | bytes 65568 | tf_op jit(solution)/shard_map/all_to_all | solution.py:172
  245.0 8.0 %convolution_convert_fusion.1 = bf16[16,2048]{1,0:T(8,128)(2,1)S(1)} fusion(bf16[2048,2048]{1,0:T(8,128)(2,1)} %param.43, bf16[16,2048]{1,0:T(8,128)(2,1)S(1)} %reshape.446, bf16[2048,2048]{1,0:T(8,128)(2,1)} %param.42), kind=kOutput, calls=%fused_computation.7 | convolution fusion | flops 268566528 | bytes 16908288 | tf_op jit(solution)/shard_map/dot_general | solution.py:175
  253.7 3.3 %all-to-all-start.1 = ((bf16[8,2,2048]{2,1,0:T(2,128)(2,1)}), bf16[8,2,2048]{2,1,0:T(2,128)(2,1)S(1)}, u32[]{:S(2)}, u32[]{:S(2)}) async-start(bf16[8,2,2048]{2,1,0:T(2,128)(2,1)} %convert_element_type.253), calls=%async_computation.1 | async-start | bytes 131072 | tf_op jit(solution)/shard_map/all_to_all | solution.py:178
  257.1 6.8 %all-to-all-done.1 = bf16[8,2,2048]{2,1,0:T(2,128)(2,1)S(1)} async-done(((bf16[8,2,2048]{2,1,0:T(2,128)(2,1)}), bf16[8,2,2048]{2,1,0:T(2,128)(2,1)S(1)}, u32[]{:S(2)}, u32[]{:S(2)}) %all-to-all-start.1) | async-done | bytes 65568 | tf_op jit(solution)/shard_map/all_to_all | solution.py:178
  (166 shorter events, 20.9 us)
Async XLA Ops:
  7.2 45.4 %copy-start = (bf16[2048,256]{1,0:T(8,128)(2,1)S(1)}, bf16[2048,256]{1,0:T(8,128)(2,1)}, u32[]{:S(2)}) copy-start(bf16[2048,256]{1,0:T(8,128)(2,1)} %param.29) | copy-start | bytes 3145732
  7.2 224.9 %all-reduce.3.cloned.1.call-start = ((), (), s32[]{:S(2)}) async-start(), calls=%async_computation.2 | async-start | bytes 524288
  7.2 10.2 %collective-permute-start = (bf16[1,4,2048]{2,1,0:T(4,128)(2,1)}, bf16[1,4,2048]{2,1,0:T(4,128)(2,1)S(1)}, u32[]{:S(2)}, u32[]{:S(2)}) collective-permute-start(bf16[1,4,2048]{2,1,0:T(4,128)(2,1)} %param.22), channel_id=1, source_target_pairs={{0,2},{2,4},{4,6},{6,8},{8,10},{10,12},{12,14},{14,0},{1,3},{3,5},... | collective-permute-start | bytes 49160 | tf_op jit(solution)/shard_map/ppermute | solution.py:29
  10.2 13.7 %collective-permute-start.4 = (bf16[1,4,2048]{2,1,0:T(4,128)(2,1)}, bf16[1,4,2048]{2,1,0:T(4,128)(2,1)S(1)}, u32[]{:S(2)}, u32[]{:S(2)}) collective-permute-start(bf16[1,4,2048]{2,1,0:T(4,128)(2,1)} %param.22), channel_id=1, source_target_pairs={{2,0},{4,2},{6,4},{8,6},{10,8},{12,10},{14,12},{0,14},{3,1},{5,3},... | collective-permute-start | bytes 49160 | tf_op jit(solution)/shard_map/ppermute | solution.py:31
  16.2 14.2 %copy-start.24 = (s32[8]{0:T(128)}, s32[8]{0:T(128)S(1)}, u32[]{:S(2)}) copy-start(s32[8]{0:T(128)S(1)} %multiply_add_fusion.20) | copy-start | bytes 100
  17.5 6.4 %collective-permute-start.1 = (bf16[1,4,2048]{2,1,0:T(4,128)(2,1)S(1)}, bf16[1,4,2048]{2,1,0:T(4,128)(2,1)S(1)}, u32[]{:S(2)}, u32[]{:S(2)}) collective-permute-start(bf16[1,4,2048]{2,1,0:T(4,128)(2,1)S(1)} %collective-permute-done), channel_id=1, source_target_pairs={{0,2},{2,4},{4,6},{6,8},{8,10},{10,12},{12,14},{14,0},{1,3},{3,5},... | collective-permute-start | bytes 49160 | tf_op jit(solution)/shard_map/ppermute | solution.py:29
  23.9 6.4 %collective-permute-start.2 = (bf16[1,4,2048]{2,1,0:T(4,128)(2,1)S(1)}, bf16[1,4,2048]{2,1,0:T(4,128)(2,1)S(1)}, u32[]{:S(2)}, u32[]{:S(2)}) collective-permute-start(bf16[1,4,2048]{2,1,0:T(4,128)(2,1)S(1)} %collective-permute-done.1), channel_id=1, source_target_pairs={{0,2},{2,4},{4,6},{6,8},{8,10},{10,12},{12,14},{14,0},{1,3},{3,5},... | collective-permute-start | bytes 49160 | tf_op jit(solution)/shard_map/ppermute | solution.py:29
  23.9 21.4 %collective-permute-start.5 = (bf16[1,4,2048]{2,1,0:T(4,128)(2,1)S(1)}, bf16[1,4,2048]{2,1,0:T(4,128)(2,1)S(1)}, u32[]{:S(2)}, u32[]{:S(2)}) collective-permute-start(bf16[1,4,2048]{2,1,0:T(4,128)(2,1)S(1)} %collective-permute-done.4), channel_id=1, source_target_pairs={{2,0},{4,2},{6,4},{8,6},{10,8},{12,10},{14,12},{0,14},{3,1},{5,3},... | collective-permute-start | bytes 49160 | tf_op jit(solution)/shard_map/ppermute | solution.py:31
  30.3 19.7 %collective-permute-start.3 = (bf16[1,4,2048]{2,1,0:T(4,128)(2,1)S(1)}, bf16[1,4,2048]{2,1,0:T(4,128)(2,1)S(1)}, u32[]{:S(2)}, u32[]{:S(2)}) collective-permute-start(bf16[1,4,2048]{2,1,0:T(4,128)(2,1)S(1)} %collective-permute-done.2), channel_id=1, source_target_pairs={{0,2},{2,4},{4,6},{6,8},{8,10},{10,12},{12,14},{14,0},{1,3},{3,5},... | collective-permute-start | bytes 49160 | tf_op jit(solution)/shard_map/ppermute | solution.py:29
  30.4 12.4 %copy-start.14 = (bf16[1,4,3,1024]{3,1,2,0:T(4,128)(2,1)S(1)}, bf16[1,4,3,1024]{3,1,2,0:T(4,128)(2,1)}, u32[]{:S(2)}) copy-start(bf16[1,4,3,1024]{3,1,2,0:T(4,128)(2,1)} %param.24) | copy-start | bytes 73732
  30.4 12.4 %copy-start.17 = (bf16[1,4,3,256]{3,1,2,0:T(4,128)(2,1)S(1)}, bf16[1,4,3,256]{3,1,2,0:T(4,128)(2,1)}, u32[]{:S(2)}) copy-start(bf16[1,4,3,256]{3,1,2,0:T(4,128)(2,1)} %param.25) | copy-start | bytes 18436
  30.4 12.4 %copy-start.20 = (s32[1,4,2]{1,2,0:T(2,128)S(1)}, s32[1,4,2]{1,2,0:T(2,128)}, u32[]{:S(2)}) copy-start(s32[1,4,2]{1,2,0:T(2,128)} %param.26) | copy-start | bytes 100
  30.4 13.6 %copy-start.28 = (u32[32]{0:T(128)S(1)}, u32[32]{0:T(128)}, u32[]{:S(2)}) copy-start(u32[32]{0:T(128)} %constant.81) | copy-start | bytes 388
  30.4 19.7 %copy-start.5 = (bf16[1,4,2048]{2,1,0:T(4,128)(2,1)S(1)}, bf16[1,4,2048]{2,1,0:T(4,128)(2,1)}, u32[]{:S(2)}) copy-start(bf16[1,4,2048]{2,1,0:T(4,128)(2,1)} %param.22) | copy-start | bytes 49156
  30.4 22.0 %copy-start.4 = (f32[2048]{0:T(1024)S(1)}, f32[2048]{0:T(1024)}, u32[]{:S(2)}) copy-start(f32[2048]{0:T(1024)} %param.27) | copy-start | bytes 24580
  42.7 10.2 %copy-start.23 = (f32[256]{0:T(256)S(1)}, f32[256]{0:T(256)}, u32[]{:S(2)}) copy-start(f32[256]{0:T(256)} %param.37) | copy-start | bytes 3076
  45.3 6.2 %collective-permute-start.6 = (bf16[1,4,2048]{2,1,0:T(4,128)(2,1)S(1)}, bf16[1,4,2048]{2,1,0:T(4,128)(2,1)S(1)}, u32[]{:S(2)}, u32[]{:S(2)}) collective-permute-start(bf16[1,4,2048]{2,1,0:T(4,128)(2,1)S(1)} %collective-permute-done.5), channel_id=1, source_target_pairs={{2,0},{4,2},{6,4},{8,6},{10,8},{12,10},{14,12},{0,14},{3,1},{5,3},... | collective-permute-start | bytes 49160 | tf_op jit(solution)/shard_map/ppermute | solution.py:31
  93.6 7.5 %copy-start.19 = (f32[1024]{0:T(1024)S(1)}, f32[1024]{0:T(1024)}, u32[]{:S(2)}) copy-start(f32[1024]{0:T(1024)} %param.35) | copy-start | bytes 12292
  101.4 5.7 %copy-start.8 = (f32[16,4,128]{2,0,1:T(8,128)S(1)}, f32[16,4,128]{2,0,1:T(8,128)}, u32[]{:S(2)}) copy-start(f32[16,4,128]{2,0,1:T(8,128)} %fusion.107) | copy-start | bytes 98308
  107.1 4.9 %copy-start.9 = (f32[16,4,128]{2,0,1:T(8,128)S(1)}, f32[16,4,128]{2,0,1:T(8,128)}, u32[]{:S(2)}) copy-start(f32[16,4,128]{2,0,1:T(8,128)} %fusion.106) | copy-start | bytes 98308
  120.5 6.7 %copy-start.11 = (f32[16,4,128]{2,0,1:T(8,128)S(1)}, f32[16,4,128]{2,0,1:T(8,128)}, u32[]{:S(2)}) copy-start(f32[16,4,128]{2,0,1:T(8,128)} %fusion.104) | copy-start | bytes 98308
  135.5 5.3 %copy-start.3 = (f32[4,16,128]{2,1,0:T(8,128)S(1)}, f32[4,16,128]{2,1,0:T(8,128)}, u32[]{:S(2)}) copy-start(f32[4,16,128]{2,1,0:T(8,128)} %convolution_bitcast_fusion) | copy-start | bytes 98308
  140.9 7.0 %copy-start.7 = (f32[16,4,128]{2,0,1:T(8,128)S(1)}, f32[16,4,128]{2,0,1:T(8,128)}, u32[]{:S(2)}) copy-start(f32[16,4,128]{2,0,1:T(8,128)} %fusion.101) | copy-start | bytes 98308
  147.9 6.7 %copy-start.26 = (f32[16]{0:T(128)S(1)}, f32[16]{0:T(128)}, u32[]{:S(2)}) copy-start(f32[16]{0:T(128)} %param.33) | copy-start | bytes 196
  156.0 76.1 %copy-start.6 = (bf16[1,4,2048]{2,1,0:T(4,128)(2,1)S(1)}, bf16[1,4,2048]{2,1,0:T(4,128)(2,1)}, u32[]{:S(2)}) copy-start(bf16[1,4,2048]{2,1,0:T(4,128)(2,1)} %param.22) | copy-start | bytes 49156
  156.0 77.0 %copy-start.16 = (f32[2048]{0:T(1024)S(1)}, f32[2048]{0:T(1024)}, u32[]{:S(2)}) copy-start(f32[2048]{0:T(1024)} %param.40) | copy-start | bytes 24580
  156.0 77.1 %copy-start.27 = (bf16[2048,8]{0,1:T(8,128)(2,1)S(1)}, bf16[2048,8]{0,1:T(8,128)(2,1)}, u32[]{:S(2)}) copy-start(bf16[2048,8]{0,1:T(8,128)(2,1)} %param.41) | copy-start | bytes 98308
  156.1 77.3 %copy-start.25 = (s32[8]{0:T(128)S(1)}, s32[8]{0:T(128)}, u32[]{:S(2)}) copy-start(s32[8]{0:T(128)} %copy-done.24) | copy-start | bytes 100
  156.1 82.0 %copy-start.22 = (s32[4,2]{1,0:T(4,128)S(1)}, s32[4,2]{1,0:T(4,128)}, u32[]{:S(2)}) copy-start(s32[4,2]{1,0:T(4,128)} %copy.177) | copy-start | bytes 100
  234.2 10.8 %all-to-all-start = ((bf16[8,2,2048]{2,1,0:T(2,128)(2,1)}), bf16[8,2,2048]{2,1,0:T(2,128)(2,1)S(1)}, u32[]{:S(2)}, u32[]{:S(2)}) async-start(bf16[8,2,2048]{2,1,0:T(2,128)(2,1)} %reshape_broadcast_in_dim_reshape.3), calls=%async_computation | async-start | bytes 131072 | tf_op jit(solution)/shard_map/all_to_all | solution.py:172
  245.0 19.0 %copy-start.18 = (pred[4,2,16]{2,1,0:T(4,128)(4,1)S(1)}, pred[4,2,16]{2,1,0:T(4,128)(4,1)}, u32[]{:S(2)}) copy-start(pred[4,2,16]{2,1,0:T(4,128)(4,1)} %eq.84) | copy-start | bytes 388
  253.7 10.2 %all-to-all-start.1 = ((bf16[8,2,2048]{2,1,0:T(2,128)(2,1)}), bf16[8,2,2048]{2,1,0:T(2,128)(2,1)S(1)}, u32[]{:S(2)}, u32[]{:S(2)}) async-start(bf16[8,2,2048]{2,1,0:T(2,128)(2,1)} %convert_element_type.253), calls=%async_computation.1 | async-start | bytes 131072 | tf_op jit(solution)/shard_map/all_to_all | solution.py:178
  (7 other events, 20.1 us)
Sparse Core Ops, SparseCore 0:
  159.9 72.1 all-reduce.2
